TPU v7x, 256 devices: a whole 4x4x8 slice. The times are simulated.
256 devices in a mesh: runs: 32 (over y, x, core), cells: 8 (over z).
Axes of the slice: x: 4, y: 4, z: 8, core: 2. Of those that a mesh axis runs over, the one named last changes fastest.
Arguments:
- train_depth: bfloat16 [16384, 32768], P('runs', 'cells'), may hold values from -6 to 6
- train_basis: bfloat16 [16384, 512], P('runs', 'cells'), may hold values from -6 to 6
- sample_basis: bfloat16 [16384, 512], P('runs', 'cells'), may hold values from -0.25 to 0.25
- gram_inverse: float32 [512, 512], replicated, may hold values from -8 to 8
Outputs:
- peak_depth: bfloat16 [16384, 32768], P('runs', 'cells')
All inputs are finite; a program needn't handle non-finite values.
Results may differ from a plain program's by a relative error of at most 0.0049.
Values may be sent and summed in bfloat16 or wider, within the bound.
No kernel may reach another device: no remote copies, remote signals or barrier semaphores. Data moves between devices by JAX's collectives and lax.ppermute only.
A program may use at most 64 MiB of HBM per device.

v0:
```python
import math
import jax
import jax.numpy as jnp
from jax import lax
from jax.sharding import PartitionSpec as P


def per_device(train_depth, train_basis, sample_basis, gram_inverse):
    terms_here = train_basis.shape[1]
    n_cells = lax.axis_size("cells")
    total_runs = train_depth.shape[0] * lax.axis_size("runs")
    norm_scale = 1.0 / math.sqrt(total_runs)
    both = jnp.concatenate([train_basis, sample_basis], axis=1).T
    both_full = lax.all_gather(both, "cells", axis=0, tiled=False)
    train_t = both_full[:, :terms_here, :].reshape(n_cells * terms_here, -1)
    sample_t = both_full[:, terms_here:, :].reshape(n_cells * terms_here, -1)
    partial_t = lax.dot_general(
        train_depth, train_t, (((0,), (1,)), ((), ())), preferred_element_type=jnp.float32
    )
    moments_t = lax.psum_scatter(partial_t, "runs", scatter_dimension=0, tiled=True) * norm_scale
    coeffs_t = lax.dot_general(
        moments_t, gram_inverse, (((1,), (1,)), ((), ())), precision=lax.Precision.HIGHEST
    ).astype(jnp.bfloat16)
    coeffs_full_t = lax.all_gather(coeffs_t, "runs", axis=0, tiled=True)
    peak_depth = lax.dot_general(
        sample_t, coeffs_full_t, (((0,), (1,)), ((), ())), preferred_element_type=jnp.float32
    ).astype(jnp.bfloat16)
    return peak_depth


def solution(mesh):
    in_specs = (P("runs", "cells"), P("runs", "cells"), P("runs", "cells"), P())
    out_specs = P("runs", "cells")
    return jax.shard_map(
        per_device, mesh=mesh, in_specs=in_specs, out_specs=out_specs, check_vma=False
    )
```

profile of v0, /device:TPU:1, one launch (start us, length us, event | category | flops | bytes accessed | tf_op | source)
XLA Modules:
  0.0 226.3 jit_solution(17582883952233589478)
XLA Ops:
  6.5 0.0 copy-start
  6.5 0.0 all-gather.6.cloned.1.call-start
  6.5 1.6 maximum_bitcast_fusion
  8.2 0.0 all-gather.6.cloned.1.call-update
  8.2 0.0 reduce-scatter.2.cloned.1.call-start
  8.2 38.1 %all-gather.6.cloned.1.call-done = bf16[1024,512]{1,0:T(8,128)(2,1)} async-done(((bf16[128,512]{1,0:T(8,128)(2,1)}), bf16[1024,512]{1,0:T(8,128)(2,1)}) %all-gather.6.cloned.1.call-update) | async-done | bytes 1048592 | tf_op jit(solution)/shard_map/all_gather | solution.py:14
  46.3 1.3 fusion.3
  47.6 7.8 %convolution_bitcast_fusion = f32[4096,512]{0,1:T(8,128)} fusion(bf16[512,512]{1,0:T(8,128)(2,1)S(1)} %bitcast.12, bf16[512,4096]{1,0:T(8,128)(2,1)} %param.4), kind=kOutput, calls=%fused_computation | convolution fusion | flops 2147483648 | bytes 13107200 | tf_op jit(solution)/shard_map/dot_general | solution.py:17
  55.4 0.0 reduce-scatter.2.cloned.1.call-update
  55.5 0.0 all-gather.4.cloned.1.call-start
  55.5 102.1 %reduce-scatter.2.cloned.1.call-done = f32[128,512]{0,1:T(8,128)} async-done(((f32[4096,512]{0,1:T(8,128)}), f32[128,512]{0,1:T(8,128)}) %reduce-scatter.2.cloned.1.call-update) | async-done | bytes 262160 | tf_op jit(solution)/shard_map/reduce_scatter | solution.py:20
  157.6 0.0 copy-done
  157.7 2.9 %convolution_convert_fusion.1 = bf16[128,512]{1,0:T(8,128)(2,1)} fusion(f32[512,512]{1,0:T(8,128)S(1)} %copy-done, f32[128,512]{0,1:T(8,128)} %reduce-scatter.2.cloned.1.call-done), kind=kOutput, calls=%fused_computation.2 | convolution fusion | flops 402784256 | bytes 1441792 | tf_op jit(solution)/shard_map/dot_general | solution.py:21
  160.5 0.0 all-gather.4.cloned.1.call-update
  160.5 52.7 %all-gather.4.cloned.1.call-done = bf16[4096,512]{1,0:T(8,128)(2,1)} async-done(((bf16[128,512]{1,0:T(8,128)(2,1)}), bf16[4096,512]{1,0:T(8,128)(2,1)}) %all-gather.4.cloned.1.call-update) | async-done | bytes 4194320 | tf_op jit(solution)/shard_map/all_gather | solution.py:24
  213.2 6.6 %convolution_convert_fusion = bf16[512,4096]{1,0:T(8,128)(2,1)} fusion(bf16[512,512]{1,0:T(8,128)(2,1)S(1)} %bitcast.14, bf16[4096,512]{1,0:T(8,128)(2,1)} %all-gather.4.cloned.1.call-done), kind=kOutput, calls=%fused_computation.1 | convolution fusion | flops 2149580800 | bytes 8912896 | tf_op jit(solution)/shard_map/dot_general | solution.py:25
Async XLA Ops:
  6.5 151.1 %copy-start = (f32[512,512]{1,0:T(8,128)S(1)}, f32[512,512]{1,0:T(8,128)}, u32[]{:S(2)}) copy-start(f32[512,512]{1,0:T(8,128)} %param.7) | copy-start | bytes 3145732
  6.5 39.8 %all-gather.6.cloned.1.call-start = ((), (), s32[]{:S(2)}) async-start(), calls=%async_computation.3 | async-start | bytes 1179648 | tf_op jit(solution)/shard_map/all_gather | solution.py:14
  8.2 149.5 %reduce-scatter.2.cloned.1.call-start = ((), (), s32[]{:S(2)}) async-start(), calls=%async_computation.1 | async-start | bytes 8650752 | tf_op jit(solution)/shard_map/reduce_scatter | solution.py:20
  55.5 157.7 %all-gather.4.cloned.1.call-start = ((), (), s32[]{:S(2)}) async-start(), calls=%async_computation.2 | async-start | bytes 4325376 | tf_op jit(solution)/shard_map/all_gather | solution.py:24
Sparse Core Ops, SparseCore 0:
  9.1 37.1 all-gather.5
  55.6 102.0 reduce-scatter.1
  160.7 52.5 all-gather.3
where the time goes:
time: 227 us; the launch traced here: 226 us
  waiting for transfers between devices  193 us (85%)
  matrix products  17.3 us (8%)
  between operations  13.1 us (6%)
    reduce_scatter x1, waiting for transfers between devices, per_device(): lax.psum_scatter(partial_t, 'runs', scatter_dimension=0, tiled=True)  102 us
    all_gather x1, waiting for transfers between devices, per_device(): coeffs_full_t = lax.all_gather(coeffs_t, 'runs', axis=0, tiled=True)  52.7 us
    all_gather x1, waiting for transfers between devices, per_device(): both_full = lax.all_gather(both, 'cells', axis=0, tiled=False)  38.1 us
    dot_general x1, matrix products, per_device(): lax.dot_general(train_depth, train_t, (((0,), (1,)), ((), ())), preferred...  7.84 us
    dot_general x1, matrix products, per_device(): lax.dot_general(sample_t, coeffs_full_t, (((0,), (1,)), ((), ())), prefer...  6.6 us
  transfers between devices with their start and end apart: 3, of which 3 were waited for; matrix products, arithmetic and copies ran while one was open for 0% of the time, Pallas kernels for 0%

commit v1 on v0

--- a/solution.py
+++ b/solution.py
@@ -3,6 +3,14 @@
 import jax.numpy as jnp
 from jax import lax
 from jax.sharding import PartitionSpec as P
+
+
+def cover_set(z, ndim_at):
+    seen = []
+    for _ in range(jax.lax.axis_size("runs")):
+        seen.append(z)
+    then = jnp.concatenate(jax.lax.all_to_all(jnp.stack(seen, 0), "runs", 0, 0), ndim_at)
+    return then
 
 
 def per_device(train_depth, train_basis, sample_basis, gram_inverse):
@@ -21,7 +29,7 @@
     coeffs_t = lax.dot_general(
         moments_t, gram_inverse, (((1,), (1,)), ((), ())), precision=lax.Precision.HIGHEST
     ).astype(jnp.bfloat16)
-    coeffs_full_t = lax.all_gather(coeffs_t, "runs", axis=0, tiled=True)
+    coeffs_full_t = cover_set(coeffs_t, 0)
     peak_depth = lax.dot_general(
         sample_t, coeffs_full_t, (((0,), (1,)), ((), ())), preferred_element_type=jnp.float32
     ).astype(jnp.bfloat16)

time: 227 us -> 230 us (1.013)
  blocking collectives: 0 us -> 57.9 us
  waiting for transfers between devices: 193 us -> 140 us
  matrix products: 17.3 us -> 14.5 us
    all_to_all x0 -> x1, blocking collectives: none -> 57.9 us  [cover_set(): jax.lax.all_to_all(jnp.stack(seen, 0), 'runs', 0, 0)]
    all_gather x1 -> x0, waiting for transfers between devices: 52.7 us -> none  [per_device(): coeffs_full_t = lax.all_gather(coeffs_t, 'runs', axis=0, tiled=True)]
  transfers between devices with their start and end apart: 3 -> 2, of which waited for: 3 -> 2; matrix products, arithmetic and copies ran while one was open for 0% -> 0% of each run, Pallas kernels for 0% -> 0%
where the time goes in v1:
time: 230 us
  waiting for transfers between devices  140 us (61%)
  blocking collectives  57.9 us (25%)
  matrix products  14.5 us (6%)
  between operations  13.4 us (6%)
    reduce_scatter x1, waiting for transfers between devices, per_device(): lax.psum_scatter(partial_t, 'runs', scatter_dimension=0, tiled=True)  102 us
    all_to_all x1, blocking collectives, cover_set(): jax.lax.all_to_all(jnp.stack(seen, 0), 'runs', 0, 0)  57.9 us
    all_gather x1, waiting for transfers between devices, per_device(): both_full = lax.all_gather(both, 'cells', axis=0, tiled=False)  38.1 us
    dot_general x1, matrix products, per_device(): lax.dot_general(train_depth, train_t, (((0,), (1,)), ((), ())), preferred...  7.84 us
  transfers between devices with their start and end apart: 2, of which 2 were waited for; matrix products, arithmetic and copies ran while one was open for 0% of the time, Pallas kernels for 0%

profile of v1, /device:TPU:1, one launch (start us, length us, event | category | flops | bytes accessed | tf_op | source)
XLA Modules:
  0.0 229.5 jit_solution(2014881393588276899)
XLA Ops:
  6.5 0.0 copy-start
  6.5 0.0 all-gather.3.cloned.1.call-start
  6.5 1.6 maximum_bitcast_fusion
  8.2 0.0 all-gather.3.cloned.1.call-update
  8.2 0.0 reduce-scatter.2.cloned.1.call-start
  8.2 38.1 %all-gather.3.cloned.1.call-done = bf16[1024,512]{1,0:T(8,128)(2,1)} async-done(((bf16[128,512]{1,0:T(8,128)(2,1)}), bf16[1024,512]{1,0:T(8,128)(2,1)}) %all-gather.3.cloned.1.call-update) | async-done | bytes 1048592 | tf_op jit(solution)/shard_map/all_gather | solution.py:22
  46.3 1.3 fusion.3
  47.6 7.8 %convolution_bitcast_fusion = f32[4096,512]{0,1:T(8,128)} fusion(bf16[512,512]{1,0:T(8,128)(2,1)S(1)} %bitcast.14, bf16[512,4096]{1,0:T(8,128)(2,1)} %param.4), kind=kOutput, calls=%fused_computation | convolution fusion | flops 2147483648 | bytes 13107200 | tf_op jit(solution)/shard_map/dot_general | solution.py:25
  55.5 0.0 reduce-scatter.2.cloned.1.call-update
  55.5 102.2 %reduce-scatter.2.cloned.1.call-done = f32[128,512]{0,1:T(8,128)} async-done(((f32[4096,512]{0,1:T(8,128)}), f32[128,512]{0,1:T(8,128)}) %reduce-scatter.2.cloned.1.call-update) | async-done | bytes 262160 | tf_op jit(solution)/shard_map/reduce_scatter | solution.py:28
  157.7 0.0 copy-done
  157.7 2.2 convolution_convert_fusion.1
  159.9 0.5 stack.2
  160.3 57.9 %all_to_all.5 = bf16[32,128,512]{2,1,0:T(8,128)(2,1)S(1)} all-to-all(bf16[32,128,512]{2,1,0:T(8,128)(2,1)S(1)} %stack.2), channel_id=1, replica_groups=mesh['runs'=32,'cells'=8] {'runs'}, dimensions={0} | all-to-all | bytes 8388608 | tf_op jit(solution)/shard_map/all_to_all | solution.py:12
  218.3 4.4 %convolution_convert_fusion = bf16[512,4096]{1,0:T(8,128)(2,1)} fusion(bf16[512,512]{1,0:T(8,128)(2,1)S(1)} %bitcast.16, bf16[4096,512]{1,0:T(8,128)(2,1)S(1)} %bitcast.13), kind=kOutput, calls=%fused_computation.1 | convolution fusion | flops 2149580800 | bytes 8912896 | tf_op jit(solution)/shard_map/dot_general | solution.py:33
Async XLA Ops:
  6.5 151.1 %copy-start = (f32[512,512]{1,0:T(8,128)S(1)}, f32[512,512]{1,0:T(8,128)}, u32[]{:S(2)}) copy-start(f32[512,512]{1,0:T(8,128)} %param.7) | copy-start | bytes 3145732
  6.5 39.8 %all-gather.3.cloned.1.call-start = ((), (), s32[]{:S(2)}) async-start(), calls=%async_computation.3 | async-start | bytes 1179648 | tf_op jit(solution)/shard_map/all_gather | solution.py:22
  8.2 149.5 %reduce-scatter.2.cloned.1.call-start = ((), (), s32[]{:S(2)}) async-start(), calls=%async_computation.2 | async-start | bytes 8650752 | tf_op jit(solution)/shard_map/reduce_scatter | solution.py:28
Sparse Core Ops, SparseCore 0:
  9.1 37.1 all-gather.2
  55.6 102.0 reduce-scatter.1
